TPU v7x, 512 devices: a whole 4x8x8 slice. The times are simulated.
512 devices in a mesh: ctx: 64 (over y, z_lo, core), dp: 8 (over z_hi, x).
Axes of the slice: x: 4, y: 8, z: 8 (z_hi: 2, z_lo: 4; z = z_hi * 4 + z_lo), core: 2. Of those that a mesh axis runs over, the one named last changes fastest.
Arguments:
- features: bfloat16 [8, 12288, 1536], P('dp', 'ctx'), may hold values from -6 to 6
- bottleneck: bfloat16 [8, 12288, 384], P('dp', 'ctx'), may hold values from -6 to 6
- node_noise: bfloat16 [8, 12288, 1536], P('dp', 'ctx'), may hold values from -6 to 6
- targets: bfloat16 [8, 12288, 1536], P('dp', 'ctx'), may hold values from -15 to 15
- entry_weight: bfloat16 [384, 1536], P('ctx'), may hold values from -0.3125 to 0.3125
- conv_filters: bfloat16 [3, 1536, 384], P(None, None, 'ctx'), may hold values from -0.09375 to 0.09375
- exit_weight: bfloat16 [384, 1536], P('ctx'), may hold values from -0.3125 to 0.3125
Outputs:
- blended: bfloat16 [8, 12288, 1536], P('dp', 'ctx')
- estimate: float32 [384, 1536], P('ctx')
All inputs are finite; a program needn't handle non-finite values.
Results may differ from a plain program's by a relative error of at most 0.015.
The roundings to bfloat16 on the way count: a program that leaves them out, or rounds other values in their place, can miss the bound.
Values may be sent and summed in bfloat16 or wider, within the bound.
No kernel may reach another device: no remote copies, remote signals or barrier semaphores. Data moves between devices by JAX's collectives and lax.ppermute only.
A program may use at most 64 MiB of HBM per device.

v0:
```python
import jax
import jax.numpy as jnp
from jax import lax
from jax.sharding import Mesh
from jax.sharding import PartitionSpec as P

DILATION = 32
NOISE_SCALE = 0.1
CTX = ("y", "zl", "c")
DP = ("zh", "x")


def _size(axes):
    n = 1
    for a in axes:
        n *= lax.axis_size(a)
    return n


def body(features, bottleneck, node_noise, targets, entry_weight, conv_filters, exit_weight):
    feats = features[0]
    bottle = bottleneck[0]
    jitter = node_noise[0]
    goal = targets[0].astype(jnp.float32)
    rows, chans = feats.shape
    bot = bottle.shape[1]
    n_ctx = _size(CTX)
    ny, nz, nc = (lax.axis_size(a) for a in CTX)
    shard = entry_weight.shape[0]
    bottle_perm = (
        bottle.reshape(rows, ny, nz, nc, shard).transpose(0, 3, 2, 1, 4).reshape(rows, bot)
    )
    summed = lax.dot_general(
        bottle_perm, jitter, (((0,), (0,)), ((), ())), preferred_element_type=jnp.float32
    )
    for axis in ("c", "zl", "y"):
        summed = lax.psum_scatter(summed, axis, scatter_dimension=0, tiled=True)
    summed_all = lax.all_gather(summed, DP, axis=0, tiled=False)
    n_dp = _size(DP)
    me_dp = lax.axis_index("zh") * lax.axis_size("x") + lax.axis_index("x")
    conv_rows = conv_filters.transpose(2, 0, 1).reshape(shard, -1)
    parts = [
        lax.dynamic_slice_in_dim(w.reshape(shard, n_dp, -1), me_dp, 1, axis=1)[:, 0]
        for w in (entry_weight, conv_rows, exit_weight)
    ]
    piece = jnp.concatenate(parts, axis=1)
    packed = lax.all_gather(piece, CTX + DP, axis=0, tiled=False)
    packed = packed.reshape(n_ctx, n_dp, shard, -1)
    cw = chans // n_dp
    w_entry = packed[..., :cw].transpose(0, 2, 1, 3).reshape(n_ctx * shard, chans)
    w_conv = packed[..., cw : 4 * cw].transpose(0, 2, 1, 3).reshape(bot, 3, chans)
    w_exit = packed[..., 4 * cw :].transpose(0, 2, 1, 3).reshape(n_ctx * shard, chans)
    spacing = DILATION
    edge_in = jnp.concatenate([feats, bottle, jitter], axis=1)
    pairs_up = [(i, i + 1) for i in range(n_ctx - 1)]
    pairs_down = [(i + 1, i) for i in range(n_ctx - 1)]
    from_prev = lax.ppermute(edge_in[rows - spacing :], CTX, pairs_up)
    from_next = lax.ppermute(edge_in[:spacing], CTX, pairs_down)
    ext = jnp.concatenate([from_prev, edge_in, from_next], axis=0)
    ext_feats = ext[:, :chans]
    ext_bottle = ext[:, chans : chans + bot]
    ext_jitter = ext[:, chans + bot :]
    baseline = ext_feats.astype(jnp.float32) + jnp.dot(
        ext_bottle, w_entry, preferred_element_type=jnp.float32
    )
    offset = ext_jitter.astype(jnp.float32) * NOISE_SCALE
    state = jnp.stack([baseline + offset, baseline - offset])
    activated = jax.nn.gelu(state).astype(jnp.bfloat16)
    mixed = None
    for k in range(3):
        term = lax.dot_general(
            activated[:, k * spacing : k * spacing + rows],
            w_conv[:, k, :],
            (((2,), (1,)), ((), ())),
            preferred_element_type=jnp.float32,
        )
        mixed = term if mixed is None else mixed + term
    inner = jax.nn.gelu(mixed).astype(jnp.bfloat16)
    outs = state[:, spacing : spacing + rows] + jnp.dot(
        inner, w_exit, preferred_element_type=jnp.float32
    )
    upper = outs[0]
    lower = outs[1]
    blended = ((upper + lower) * 0.5).astype(jnp.bfloat16)[None]
    local_gap = jnp.sum((upper - lower) * (upper + lower - 2.0 * goal)) / (rows * n_ctx * chans)
    slots = jnp.zeros((n_dp,), jnp.float32).at[me_dp].set(local_gap)
    gaps = lax.psum(slots, CTX + DP)
    factors = gaps / (2.0 * NOISE_SCALE)
    estimate = jnp.sum(factors[:, None, None] * summed_all, axis=0)
    return (blended, estimate)


def solution(mesh):
    ctx_n, dp_n = mesh.devices.shape
    devices = mesh.devices.reshape(8, ctx_n // 16, 2, dp_n // 4, 4)
    fine = Mesh(devices, CTX + DP)
    return jax.shard_map(
        body,
        mesh=fine,
        in_specs=(
            P(DP, CTX, None),
            P(DP, CTX, None),
            P(DP, CTX, None),
            P(DP, CTX, None),
            P(CTX, None),
            P(None, None, CTX),
            P(CTX, None),
        ),
        out_specs=(P(DP, CTX, None), P(CTX, None)),
        check_vma=False,
    )
```

profile of v0, /device:TPU:1, one launch (start us, length us, event | category | flops | bytes accessed | tf_op | source)
XLA Modules:
  0.0 1673.8 jit_solution(16459171354127405826)
XLA Ops:
  9.4 1.9 fusion.43
  11.4 25.1 %reduce-scatter.5.cloned.1.call-done = f32[192,1536]{1,0:T(8,128)} async-done(((f32[384,1536]{1,0:T(8,128)}), f32[192,1536]{1,0:T(8,128)}) %reduce-scatter.5.cloned.1.call-update) | async-done | bytes 1179664 | tf_op jit(solution)/shard_map/reduce_scatter | solution.py:37
  37.8 1.9 collective-permute-start.1
  39.7 3.6 collective-permute-start
  45.3 32.1 %reduce-scatter.7.cloned.1.call-done = f32[48,1536]{1,0:T(8,128)} async-done(((f32[192,1536]{1,0:T(8,128)}), f32[48,1536]{1,0:T(8,128)}) %reduce-scatter.7.cloned.1.call-update) | async-done | bytes 294928 | tf_op jit(solution)/shard_map/reduce_scatter | solution.py:37
  77.4 17.1 %fusion = f32[8,1536]{1,0:T(8,128)S(1)} fusion(f32[48,1536]{1,0:T(8,128)} %reduce-scatter.7.cloned.1.call-done), kind=kCustom, calls=%all-reduce-scatter | all-reduce-scatter fusion | flops 98305 | bytes 346112
  94.6 2.1 collective-permute-start.2
  96.7 3.5 collective-permute-start.3
  100.2 1.4 pad_maximum_fusion.1
  101.9 1356.0 %all-gather.6.cloned.1.call-done = bf16[512,6,960]{2,1,0:T(8,128)(2,1)} async-done(((bf16[1,6,960]{2,1,0:T(8,128)(2,1)}), bf16[512,6,960]{2,1,0:T(8,128)(2,1)}) %all-gather.6.cloned.1.call-update) | async-done | bytes 5898256 | tf_op jit(solution)/shard_map/all_gather | solution.py:47
  1457.9 6.9 copy.60
  1465.1 4.1 slice_bitcast_fusion
  1469.2 1.3 copy.35
  1470.4 3.8 reshape.88
  1475.5 3.8 reshape.71
  1479.2 4.4 copy.31
  1483.6 12.4 reshape.72
  1496.0 12.1 fusion.49
  1508.1 1.8 subtract_bitcast_fusion
  1512.3 1.6 convolution_add_fusion.2
  1513.9 5.6 convolution_add_fusion
  1519.5 3.4 multiply_reduce_fusion
  1523.6 37.9 %all-gather.3 = f32[8,6,1536]{2,1,0:T(8,128)S(1)} all-gather(f32[1,6,1536]{2,1,0:T(8,128)S(1)} %dynamic-slice_bitcast_fusion), channel_id=3, replica_groups=mesh['y'=8,'zl'=4,'c'=2,'zh'=2,'x'=4] {'zh','x'}, dimensions={0}, use_global_device_ids=true | all-gather | bytes 331776 | tf_op jit(solution)/shard_map/all_gather | solution.py:38
  1561.5 104.2 %psum.7 = f32[8]{0:T(128)S(1)} all-reduce(f32[8]{0:T(128)S(1)} %scatter.4), channel_id=1, replica_groups=mesh['y'=8,'zl'=4,'c'=2,'zh'=2,'x'=4] {'y','zl','c','zh','x'}, use_global_device_ids=true, to_apply=%region_1.0 | all-reduce | flops 8 | bytes 64 | tf_op jit(solution)/shard_map/psum | solution.py:87
  (59 shorter events, 9.0 us)
Async XLA Ops:
  8.0 1.4 copy-start
  8.0 28.4 %reduce-scatter.5.cloned.1.call-start = ((), (), s32[]{:S(2)}) async-start(), calls=%async_computation.2 | async-start | bytes 3538944 | tf_op jit(solution)/shard_map/reduce_scatter | solution.py:37
  11.3 25.2 %copy-start.9 = (bf16[6,1536]{1,0:T(8,128)(2,1)S(1)}, bf16[6,1536]{1,0:T(8,128)(2,1)}, u32[]{:S(2)}) copy-start(bf16[6,1536]{1,0:T(8,128)(2,1)} %param.15) | copy-start | bytes 55300
  11.3 25.3 %copy-start.10 = (bf16[6,1536]{1,0:T(8,128)(2,1)S(1)}, bf16[6,1536]{1,0:T(8,128)(2,1)}, u32[]{:S(2)}) copy-start(bf16[6,1536]{1,0:T(8,128)(2,1)} %param.13) | copy-start | bytes 55300
  11.3 25.5 %copy-start.8 = (bf16[3,1536,6]{1,2,0:T(8,128)(2,1)S(1)}, bf16[3,1536,6]{1,2,0:T(8,128)(2,1)}, u32[]{:S(2)}) copy-start(bf16[3,1536,6]{1,2,0:T(8,128)(2,1)} %param.14) | copy-start | bytes 165892
  11.3 26.4 %copy-start.1 = (bf16[1,192,1536]{2,1,0:T(8,128)(2,1)S(1)}, bf16[1,192,1536]{2,1,0:T(8,128)(2,1)}, u32[]{:S(2)}) copy-start(bf16[1,192,1536]{2,1,0:T(8,128)(2,1)} %param.9) | copy-start | bytes 1769476
  11.3 26.4 %copy-start.4 = (bf16[1,192,384]{2,1,0:T(8,128)(2,1)S(1)}, bf16[1,192,384]{2,1,0:T(8,128)(2,1)}, u32[]{:S(2)}) copy-start(bf16[1,192,384]{2,1,0:T(8,128)(2,1)} %param.10) | copy-start | bytes 442372
  11.3 66.1 %reduce-scatter.7.cloned.1.call-start = ((), (), s32[]{:S(2)}) async-start(), calls=%async_computation.3 | async-start | bytes 1474560 | tf_op jit(solution)/shard_map/reduce_scatter | solution.py:37
  36.5 1421.4 %all-gather.6.cloned.1.call-start = ((), (), s32[]{:S(2)}) async-start(), calls=%async_computation.4 | async-start | bytes 8404992 | tf_op jit(solution)/shard_map/all_gather | solution.py:47
  37.8 62.4 %collective-permute-start.1 = (bf16[32,3456]{1,0:T(8,128)(2,1)S(1)}, bf16[32,3456]{1,0:T(8,128)(2,1)S(1)}, u32[]{:S(2)}, u32[]{:S(2)}) collective-permute-start(bf16[32,3456]{1,0:T(8,128)(2,1)S(1)} %get-tuple-element.24), channel_id=1, source_target_pairs={{8,0},{16,8},{24,16},{32,24},{40,32},{48,40},{56,48},{64,56},{72,6... | collective-permute-start | bytes 663560 | tf_op jit(solution)/shard_map/ppermute | solution.py:58
  39.7 60.5 %collective-permute-start = (bf16[32,3456]{1,0:T(8,128)(2,1)S(1)}, bf16[32,3456]{1,0:T(8,128)(2,1)S(1)}, u32[]{:S(2)}, u32[]{:S(2)}) collective-permute-start(bf16[32,3456]{1,0:T(8,128)(2,1)S(1)} %get-tuple-element.23), channel_id=1, source_target_pairs={{0,8},{8,16},{16,24},{24,32},{32,40},{40,48},{48,56},{56,64},{64,7... | collective-permute-start | bytes 663560 | tf_op jit(solution)/shard_map/ppermute | solution.py:57
  94.6 7.0 collective-permute-start.2
  96.7 4.9 collective-permute-start.3
  1496.0 12.1 copy-start.3
  1509.9 1.1 copy-start.2
  1511.0 1.2 copy-start.5
  1512.3 1.6 copy-start.6
  1513.9 5.6 copy-start.7
Sparse Core Ops, SparseCore 0:
  11.6 24.7 reduce-scatter.4
  39.5 37.8 reduce-scatter.6
Sparse Core Ops, SparseCore 1:
  39.7 1418.1 all-gather.5
where the time goes:
time: 1670 us
  waiting for transfers between devices  1410 us (84%)
  blocking collectives  159 us (10%)
  local copies, waits for them, and re-layouts  54.3 us (3%)
  between operations  17.1 us (1%)
    all_gather x1, waiting for transfers between devices, body(): packed = lax.all_gather(piece, CTX + DP, axis=0, tiled=False)  1360 us
    psum x1, blocking collectives, body(): gaps = lax.psum(slots, CTX + DP)  104 us
    reduce_scatter x2, waiting for transfers between devices, body(): summed = lax.psum_scatter(summed, axis, scatter_dimension=0, tiled=True)  57.2 us
    all_gather x1, blocking collectives, body(): summed_all = lax.all_gather(summed, DP, axis=0, tiled=False)  37.9 us
  transfers between devices with their start and end apart: 7, of which 3 were waited for; matrix products, arithmetic and copies ran while one was open for 1% of the time, Pallas kernels for 0%

commit v1 on v0

--- a/solution.py
+++ b/solution.py
@@ -84,7 +84,9 @@
     blended = ((upper + lower) * 0.5).astype(jnp.bfloat16)[None]
     local_gap = jnp.sum((upper - lower) * (upper + lower - 2.0 * goal)) / (rows * n_ctx * chans)
     slots = jnp.zeros((n_dp,), jnp.float32).at[me_dp].set(local_gap)
-    gaps = lax.psum(slots, CTX + DP)
+    mesh_axis = CTX + DP
+    pieces = lax.all_gather(slots, mesh_axis)
+    gaps = jnp.sum(pieces, axis=0)
     factors = gaps / (2.0 * NOISE_SCALE)
     estimate = jnp.sum(factors[:, None, None] * summed_all, axis=0)
     return (blended, estimate)

time: 1670 us -> 2950 us (1.77)
  blocking collectives: 159 us -> 1470 us
  waiting for transfers between devices: 1410 us -> 1370 us
    all_gather x0 -> x1, blocking collectives: none -> 1410 us  [body(): pieces = lax.all_gather(slots, mesh_axis)]
    psum x1 -> x0, blocking collectives: 104 us -> none  [body(): gaps = lax.psum(slots, CTX + DP)]
    all_gather x1, waiting for transfers between devices: 1360 us -> 1320 us  [body(): packed = lax.all_gather(piece, CTX + DP, axis=0, tiled=False)]
where the time goes in v1:
time: 2950 us
  blocking collectives  1470 us (50%)
  waiting for transfers between devices  1370 us (46%)
  local copies, waits for them, and re-layouts  53.9 us (2%)
    all_gather x1, blocking collectives, body(): pieces = lax.all_gather(slots, mesh_axis)  1410 us
    all_gather x1, waiting for transfers between devices, body(): packed = lax.all_gather(piece, CTX + DP, axis=0, tiled=False)  1320 us
  transfers between devices with their start and end apart: 7, of which 3 were waited for; matrix products, arithmetic and copies ran while one was open for 1% of the time, Pallas kernels for 0%

profile of v1, /device:TPU:1, one launch (start us, length us, event | category | flops | bytes accessed | tf_op | source)
XLA Modules:
  0.0 2945.7 jit_solution(18153754981604052314)
XLA Ops:
  9.4 1.9 fusion.43
  11.4 25.1 reduce-scatter.5.cloned.1.call-done
  37.8 1.9 collective-permute-start.1
  39.7 3.6 collective-permute-start
  45.3 32.1 %reduce-scatter.7.cloned.1.call-done = f32[48,1536]{1,0:T(8,128)} async-done(((f32[192,1536]{1,0:T(8,128)}), f32[48,1536]{1,0:T(8,128)}) %reduce-scatter.7.cloned.1.call-update) | async-done | bytes 294928 | tf_op jit(solution)/shard_map/reduce_scatter | solution.py:37
  77.4 17.1 fusion
  94.6 2.1 collective-permute-start.2
  96.7 3.5 collective-permute-start.3
  100.2 1.4 pad_maximum_fusion.1
  101.9 39.9 %all-gather.4 = f32[8,6,1536]{2,1,0:T(8,128)} all-gather(f32[1,6,1536]{2,1,0:T(8,128)S(1)} %dynamic-slice_bitcast_fusion), channel_id=3, replica_groups=mesh['y'=8,'zl'=4,'c'=2,'zh'=2,'x'=4] {'zh','x'}, dimensions={0}, use_global_device_ids=true | all-gather | bytes 331776 | tf_op jit(solution)/shard_map/all_gather | solution.py:38
  141.8 1316.1 %all-gather.7.cloned.1.call-done = bf16[512,6,960]{2,1,0:T(8,128)(2,1)} async-done(((bf16[1,6,960]{2,1,0:T(8,128)(2,1)}), bf16[512,6,960]{2,1,0:T(8,128)(2,1)}) %all-gather.7.cloned.1.call-update) | async-done | bytes 5898256 | tf_op jit(solution)/shard_map/all_gather | solution.py:47
  1457.9 6.9 copy.60
  1465.1 4.1 slice_bitcast_fusion
  1470.4 3.7 reshape.95
  1474.2 1.3 copy.30
  1475.5 3.8 reshape.74
  1479.2 4.4 copy.31
  1483.6 12.4 reshape.75
  1496.0 11.9 fusion.49
  1507.9 1.8 subtract_bitcast_fusion
  1512.0 1.6 convolution_add_fusion.2
  1513.6 5.6 convolution_add_fusion
  1519.2 3.4 multiply_reduce_fusion
  1523.3 1413.7 %all-gather.3 = f32[512,1,8]{2,1,0:T(1,128)S(1)} all-gather(f32[1,1,8]{2,1,0:T(1,128)S(1)} %scatter.6), channel_id=1, replica_groups=mesh['y'=8,'zl'=4,'c'=2,'zh'=2,'x'=4] {'y','zl','c','zh','x'}, dimensions={0}, use_global_device_ids=true | all-gather | bytes 16416 | tf_op jit(solution)/shard_map/all_gather | solution.py:88
  (62 shorter events, 9.5 us)
Async XLA Ops:
  8.0 1.4 copy-start
  8.0 28.4 reduce-scatter.5.cloned.1.call-start
  11.3 25.2 copy-start.10
  11.3 25.3 copy-start.11
  11.3 25.5 copy-start.9
  11.3 26.4 copy-start.1
  11.3 26.4 copy-start.4
  11.3 66.1 %reduce-scatter.7.cloned.1.call-start = ((), (), s32[]{:S(2)}) async-start(), calls=%async_computation.3 | async-start | bytes 1474560 | tf_op jit(solution)/shard_map/reduce_scatter | solution.py:37
  36.5 1421.4 %all-gather.7.cloned.1.call-start = ((), (), s32[]{:S(2)}) async-start(), calls=%async_computation.4 | async-start | bytes 8404992 | tf_op jit(solution)/shard_map/all_gather | solution.py:47
  37.8 62.4 %collective-permute-start.1 = (bf16[32,3456]{1,0:T(8,128)(2,1)S(1)}, bf16[32,3456]{1,0:T(8,128)(2,1)S(1)}, u32[]{:S(2)}, u32[]{:S(2)}) collective-permute-start(bf16[32,3456]{1,0:T(8,128)(2,1)S(1)} %get-tuple-element.24), channel_id=1, source_target_pairs={{8,0},{16,8},{24,16},{32,24},{40,32},{48,40},{56,48},{64,56},{72,6... | collective-permute-start | bytes 663560 | tf_op jit(solution)/shard_map/ppermute | solution.py:58
  39.7 60.5 %collective-permute-start = (bf16[32,3456]{1,0:T(8,128)(2,1)S(1)}, bf16[32,3456]{1,0:T(8,128)(2,1)S(1)}, u32[]{:S(2)}, u32[]{:S(2)}) collective-permute-start(bf16[32,3456]{1,0:T(8,128)(2,1)S(1)} %get-tuple-element.23), channel_id=1, source_target_pairs={{0,8},{8,16},{16,24},{24,32},{32,40},{40,48},{48,56},{56,64},{64,7... | collective-permute-start | bytes 663560 | tf_op jit(solution)/shard_map/ppermute | solution.py:57
  94.6 7.0 collective-permute-start.2
  96.7 4.9 collective-permute-start.3
  1496.0 11.9 copy-start.3
  1509.6 1.1 copy-start.2
  1510.8 1.2 copy-start.6
  1512.0 1.6 copy-start.7
  1513.6 5.6 copy-start.8
  1519.2 1418.4 %copy-start.5 = (f32[8,6,1536]{2,1,0:T(8,128)S(1)}, f32[8,6,1536]{2,1,0:T(8,128)}, u32[]{:S(2)}) copy-start(f32[8,6,1536]{2,1,0:T(8,128)} %all-gather.4) | copy-start | bytes 884740
Sparse Core Ops, SparseCore 0:
  11.6 24.7 reduce-scatter.4
  39.5 37.8 reduce-scatter.6
Sparse Core Ops, SparseCore 1:
  39.7 1418.1 all-gather.6
